TPU v7x, 128 devices: a whole 4x4x4 slice. The times are simulated.
128 devices in a mesh: row: 4 (over z), col: 32 (over x, y, core).
Axes of the slice: x: 4, y: 4, z: 4, core: 2. Of those that a mesh axis runs over, the one named last changes fastest.
Arguments:
- matrix_real: bfloat16 [512, 16384], P('col', 'row'), may hold values from -0.25 to 0.25
- matrix_imag: bfloat16 [512, 16384], P('col', 'row'), may hold values from -0.25 to 0.25
- valence_index: int32 [512], P('col'), may hold values from 0 to 15
- conduction_index: int32 [512], P('col'), may hold values from 0 to 31
- valence_energy: float32 [16], replicated, may hold values from -1.5 to -0.1
- conduction_energy: float32 [32], replicated, may hold values from 0.1 to 2
- frequency: float32 [2], replicated, may hold values from 0.2 to 2
Outputs:
- chi_real: bfloat16 [2, 16384, 16384], P(None, 'row', 'col')
- chi_imag: bfloat16 [2, 16384, 16384], P(None, 'row', 'col')
All inputs are finite; a program needn't handle non-finite values.
Results may differ from a plain program's by a relative error of at most 0.005.
Values may be sent and summed in bfloat16 or wider, within the bound.
No kernel may reach another device: no remote copies, remote signals or barrier semaphores. Data moves between devices by JAX's collectives and lax.ppermute only.
A program may use at most 192 MiB of HBM per device.

v0:
```python
import jax
import jax.numpy as jnp
from jax import lax
from jax.sharding import PartitionSpec as P


def lookup(indices, table):
    count = table.shape[0]
    picks = indices[:, None] == lax.broadcasted_iota(jnp.int32, (1, count), 1)
    return jnp.sum(jnp.where(picks, table[None, :], 0.0), axis=1)


def contract(left_side, right_side):
    return lax.dot_general(
        left_side, right_side, (((0,), (0,)), ((), ())), preferred_element_type=jnp.float32
    )


CHUNKS = 4


def on_device(
    matrix_real,
    matrix_imag,
    valence_index,
    conduction_index,
    valence_energy,
    conduction_energy,
    frequency,
):
    ncol = lax.psum(1, "col")
    local_pairs, local_g = matrix_real.shape
    pairs = local_pairs * ncol
    both = jnp.stack([matrix_real, matrix_imag])
    bands = jnp.stack([valence_index, conduction_index]).astype(jnp.float32)
    all_bands = lax.all_gather(bands, "col", axis=1, tiled=True).astype(jnp.int32)
    gap = lookup(all_bands[1], conduction_energy) - lookup(all_bands[0], valence_energy)
    spread = lax.all_gather(both, "row", axis=2, tiled=True)
    spread = spread.reshape(2, local_pairs, ncol, -1)
    column = lax.all_to_all(spread, "col", split_axis=2, concat_axis=1, tiled=True)
    width = column.shape[-1]
    wide = column.reshape(2, pairs, width).astype(jnp.float32)
    right_real = []
    right_imag = []
    for index in range(frequency.shape[0]):
        omega = frequency[index]
        weight = 4.0 * gap / (gap * gap + omega * omega)
        scaled_real = (weight[:, None] * wide[0]).astype(jnp.bfloat16)
        scaled_imag = (weight[:, None] * wide[1]).astype(jnp.bfloat16)
        right_real.append(jnp.concatenate([-scaled_real, -scaled_imag], axis=0))
        right_imag.append(jnp.concatenate([-scaled_imag, scaled_real], axis=0))
    step = local_g // CHUNKS
    real_parts = [[] for _ in right_real]
    imag_parts = [[] for _ in right_real]
    for chunk in range(CHUNKS):
        piece = both[:, :, chunk * step : (chunk + 1) * step]
        left = lax.all_gather(piece, "col", axis=1, tiled=True).reshape(2 * pairs, step)
        for index in range(len(right_real)):
            real_parts[index].append(contract(left, right_real[index]).astype(jnp.bfloat16))
            imag_parts[index].append(contract(left, right_imag[index]).astype(jnp.bfloat16))
    chi_real = jnp.stack([jnp.concatenate(p, axis=0) for p in real_parts])
    chi_imag = jnp.stack([jnp.concatenate(p, axis=0) for p in imag_parts])
    return (chi_real, chi_imag)


def solution(mesh):
    placed = (P("col", "row"), P("col", "row"), P("col"), P("col"), P(), P(), P())
    return jax.shard_map(
        on_device,
        mesh=mesh,
        in_specs=placed,
        out_specs=(P(None, "row", "col"), P(None, "row", "col")),
        check_vma=False,
    )
```

profile of v0, /device:TPU:1, one launch (start us, length us, event | category | flops | bytes accessed | tf_op | source)
XLA Modules:
  0.0 271.8 jit_solution(17406845412309366294)
XLA Ops:
  7.2 0.0 all-gather.9.cloned.1.call-start
  7.2 1.7 pad_maximum_fusion.6
  8.9 0.0 all-gather.9.cloned.1.call-update
  8.9 0.0 all-gather.11.cloned.1.call-start
  9.0 1.6 fusion.6
  10.6 0.0 all-gather.11.cloned.1.call-update
  10.6 0.0 all-gather.7.cloned.1.call-start
  10.6 0.7 all-gather.7.cloned.1.call-update
  11.3 0.0 all-gather.13.cloned.1.call-start
  11.4 0.5 all-gather.13.cloned.1.call-update
  11.9 24.9 %all-gather.9.cloned.1.call-done = bf16[2,16,16384]{2,1,0:T(8,128)(2,1)} async-done(((bf16[2,16,4096]{2,1,0:T(8,128)(2,1)}), bf16[2,16,16384]{2,1,0:T(8,128)(2,1)}) %all-gather.9.cloned.1.call-update) | async-done | bytes 1048592 | tf_op jit(solution)/shard_map/all_gather | solution.py:38
  36.8 2.4 copy.26
  39.2 8.4 %all-to-all-start = ((bf16[2,16,32,512]{3,1,0,2:T(8,128)(2,1)}), bf16[2,16,32,512]{3,1,0,2:T(8,128)(2,1)S(1)}, u32[]{:S(2)}, u32[]{:S(2)}) async-start(bf16[2,16,32,512]{3,1,0,2:T(8,128)(2,1)} %bitcast.71), calls=%async_computation | async-start | bytes 2097152 | tf_op jit(solution)/shard_map/all_to_all | solution.py:40
  47.6 0.0 all-gather.15.cloned.1.call-start
  47.7 0.5 all-gather.15.cloned.1.call-update
  48.2 0.0 copy-done.12
  48.2 0.6 fusion.17
  51.3 0.0 copy-done.15
  51.3 0.0 copy-done.16
  51.3 29.0 %all-gather = f32[32,16,2]{1,2,0:T(2,128)S(1)} all-gather(f32[1,16,2]{1,2,0:T(2,128)S(1)} %fusion.10), channel_id=1, replica_groups=mesh['row'=4,'col'=32] {'col'}, dimensions={0}, use_global_device_ids=true | all-gather | bytes 4224 | tf_op jit(solution)/shard_map/all_gather | solution.py:36
  80.3 0.1 copy.19
  80.4 0.1 copy.20
  80.5 0.1 reshape.57
  80.6 0.1 select_reduce_fusion.1
  80.7 0.1 select_reduce_fusion
  80.8 0.0 all-to-all-done
  80.8 0.3 convert_bitcast_fusion
  81.1 0.2 fusion.15
  81.3 1.4 fusion.5
  82.7 5.7 %all-gather.11.cloned.1.call-done = bf16[2,512,1024]{2,1,0:T(8,128)(2,1)} async-done(((bf16[2,16,1024]{2,1,0:T(8,128)(2,1)}), bf16[2,512,1024]{2,1,0:T(8,128)(2,1)}) %all-gather.11.cloned.1.call-update) | async-done | bytes 2097168 | tf_op jit(solution)/shard_map/all_gather | solution.py:57
  88.4 3.8 %convolution_convert_fusion.10 = bf16[1024,512]{1,0:T(8,128)(2,1)} fusion(bf16[1024,1024]{1,0:T(8,128)(2,1)} %bitcast.82, bf16[512,512]{1,0:T(8,128)(2,1)S(1)} %get-tuple-element.11, bf16[512,512]{1,0:T(8,128)(2,1)S(1)} %get-tuple-element.16), kind=kOutput, calls=%fused_computation.17 | convolution fusion | flops 1076363264 | bytes 4194304 | tf_op jit(solution)/shard_map/dot_general | solution.py:14
  92.3 41.5 %all-gather.7.cloned.1.call-done = bf16[2,512,1024]{2,1,0:T(8,128)(2,1)} async-done(((bf16[2,16,1024]{2,1,0:T(8,128)(2,1)}), bf16[2,512,1024]{2,1,0:T(8,128)(2,1)}) %all-gather.7.cloned.1.call-update) | async-done | bytes 2097168 | tf_op jit(solution)/shard_map/all_gather | solution.py:57
  133.8 4.0 %convolution_convert_fusion.11 = bf16[1024,512]{1,0:T(8,128)(2,1)} fusion(bf16[1024,1024]{1,0:T(8,128)(2,1)} %bitcast.86, bf16[512,512]{1,0:T(8,128)(2,1)S(1)} %get-tuple-element.11, bf16[512,512]{1,0:T(8,128)(2,1)S(1)} %get-tuple-element.16), kind=kOutput, calls=%fused_computation.18 | convolution fusion | flops 1076363264 | bytes 4194304 | tf_op jit(solution)/shard_map/dot_general | solution.py:14
  137.7 0.0 copy-done.19
  137.8 0.0 copy-start.17
  137.8 1.3 convolution_convert_fusion.3
  139.1 0.3 copy-done.17
  139.3 2.5 convolution_convert_fusion.2
  141.9 37.1 %all-gather.13.cloned.1.call-done = bf16[2,512,1024]{2,1,0:T(8,128)(2,1)} async-done(((bf16[2,16,1024]{2,1,0:T(8,128)(2,1)}), bf16[2,512,1024]{2,1,0:T(8,128)(2,1)}) %all-gather.13.cloned.1.call-update) | async-done | bytes 2097168 | tf_op jit(solution)/shard_map/all_gather | solution.py:57
  179.0 4.2 %convolution_convert_fusion.9 = bf16[1024,512]{1,0:T(8,128)(2,1)} fusion(bf16[1024,1024]{1,0:T(8,128)(2,1)} %bitcast.90, bf16[512,512]{1,0:T(8,128)(2,1)} %copy-done.5, bf16[512,512]{1,0:T(8,128)(2,1)} %copy-done.11), kind=kOutput, calls=%fused_computation.16 | convolution fusion | flops 1076363264 | bytes 4194304 | tf_op jit(solution)/shard_map/dot_general | solution.py:14
  183.2 2.3 convolution_convert_fusion.1
  185.5 38.7 %all-gather.15.cloned.1.call-done = bf16[2,512,1024]{2,1,0:T(8,128)(2,1)} async-done(((bf16[2,16,1024]{2,1,0:T(8,128)(2,1)}), bf16[2,512,1024]{2,1,0:T(8,128)(2,1)}) %all-gather.15.cloned.1.call-update) | async-done | bytes 2097168 | tf_op jit(solution)/shard_map/all_gather | solution.py:57
  224.2 3.3 %convolution_convert_fusion.8 = bf16[1024,512]{1,0:T(8,128)(2,1)S(1)} fusion(bf16[1024,1024]{1,0:T(8,128)(2,1)} %bitcast.94, bf16[512,512]{1,0:T(8,128)(2,1)} %copy-done.5, bf16[512,512]{1,0:T(8,128)(2,1)} %copy-done.11), kind=kOutput, calls=%fused_computation.15 | convolution fusion | flops 1076363264 | bytes 4194304 | tf_op jit(solution)/shard_map/dot_general | solution.py:14
  227.5 0.0 copy-done.7
  227.5 0.0 copy-done.10
  227.5 0.0 copy-done.23
  227.5 0.0 copy-start.3
  227.5 0.0 copy-start.18
  227.5 2.3 convolution_convert_fusion
  229.8 1.3 convolution_convert_fusion.14
  231.1 0.3 copy-done.22
  231.4 1.3 convolution_convert_fusion.13
  232.7 2.5 convolution_convert_fusion.6
  235.2 2.3 convolution_convert_fusion.5
  237.5 1.3 convolution_convert_fusion.12
  238.8 2.4 convolution_convert_fusion.4
  241.2 2.3 convolution_convert_fusion.7
  243.4 1.3 convolution_convert_fusion.15
  244.7 0.2 copy-done.1
  245.0 0.3 copy-done.2
  245.3 2.8 %maximum_bitcast_fusion = (bf16[1,4096,512]{2,1,0:T(8,128)(2,1)S(1)}, bf16[1,4096,512]{2,1,0:T(8,128)(2,1)}) fusion(bf16[1024,512]{1,0:T(8,128)(2,1)S(1)} %convolution_convert_fusion.12, bf16[1024,512]{1,0:T(8,128)(2,1)S(1)} %convolution_convert_fusion.13, bf16[1024,512]{1,0:T(8,128)(2,1)S(1)} %convolution_convert_fusion.14, ...), kind=kLoop, calls=%fused_computation.2 | loop fusion | flops 33554432 | bytes 16777216 | tf_op jit(solution)/shard_map/stack | solution.py:61
  248.1 6.3 %pad_maximum_fusion = bf16[2,4096,512]{2,1,0:T(8,128)(2,1)} fusion(bf16[1,4096,512]{2,1,0:T(8,128)(2,1)} %get-tuple-element.27, bf16[1,4096,512]{2,1,0:T(8,128)(2,1)S(1)} %get-tuple-element.26), kind=kLoop, calls=%fused_computation | loop fusion | flops 4194304 | bytes 16777216 | tf_op jit(solution)/shard_map/stack | solution.py:61
  254.5 4.4 %maximum_bitcast_fusion.2 = (bf16[1,4096,512]{2,1,0:T(8,128)(2,1)S(1)}, bf16[1,4096,512]{2,1,0:T(8,128)(2,1)}) fusion(bf16[1024,512]{1,0:T(8,128)(2,1)} %convolution_convert_fusion.4, bf16[1024,512]{1,0:T(8,128)(2,1)} %convolution_convert_fusion.5, bf16[1024,512]{1,0:T(8,128)(2,1)} %convolution_convert_fusion.6, ...), kind=kLoop, calls=%fused_computation.4 | loop fusion | flops 33554432 | bytes 16777216 | tf_op jit(solution)/shard_map/stack | solution.py:62
  258.9 6.3 %pad_maximum_fusion.1 = bf16[2,4096,512]{2,1,0:T(8,128)(2,1)} fusion(bf16[1,4096,512]{2,1,0:T(8,128)(2,1)} %get-tuple-element.29, bf16[1,4096,512]{2,1,0:T(8,128)(2,1)S(1)} %get-tuple-element.28), kind=kLoop, calls=%fused_computation.1 | loop fusion | flops 4194304 | bytes 16777216 | tf_op jit(solution)/shard_map/stack | solution.py:62
  (38 shorter events, 0.1 us)
Async XLA Ops:
  7.2 29.6 %all-gather.9.cloned.1.call-start = ((), (), s32[]{:S(2)}) async-start(), calls=%async_computation.2 | async-start | bytes 1310720 | tf_op jit(solution)/shard_map/all_gather | solution.py:38
  8.9 79.5 %all-gather.11.cloned.1.call-start = ((), (), s32[]{:S(2)}) async-start(), calls=%async_computation.3 | async-start | bytes 2162688 | tf_op jit(solution)/shard_map/all_gather | solution.py:57
  10.6 123.2 %all-gather.7.cloned.1.call-start = ((), (), s32[]{:S(2)}) async-start(), calls=%async_computation.1 | async-start | bytes 2162688 | tf_op jit(solution)/shard_map/all_gather | solution.py:57
  11.3 167.7 %all-gather.13.cloned.1.call-start = ((), (), s32[]{:S(2)}) async-start(), calls=%async_computation.4 | async-start | bytes 2162688 | tf_op jit(solution)/shard_map/all_gather | solution.py:57
  36.8 11.5 %copy-start.12 = (f32[2]{0:T(128)S(1)}, f32[2]{0:T(128)}, u32[]{:S(2)}) copy-start(f32[2]{0:T(128)} %param.13) | copy-start | bytes 28
  36.8 14.5 %copy-start.15 = (s32[16]{0:T(128)S(1)}, s32[16]{0:T(128)}, u32[]{:S(2)}) copy-start(s32[16]{0:T(128)} %param.10) | copy-start | bytes 196
  36.8 14.5 %copy-start.16 = (s32[16]{0:T(128)S(1)}, s32[16]{0:T(128)}, u32[]{:S(2)}) copy-start(s32[16]{0:T(128)} %param.9) | copy-start | bytes 196
  36.8 43.8 %copy-start.13 = (f32[16]{0:T(128)S(1)}, f32[16]{0:T(128)}, u32[]{:S(2)}) copy-start(f32[16]{0:T(128)} %param.11) | copy-start | bytes 196
  36.8 43.9 %copy-start.14 = (f32[32]{0:T(128)S(1)}, f32[32]{0:T(128)}, u32[]{:S(2)}) copy-start(f32[32]{0:T(128)} %param.12) | copy-start | bytes 388
  39.2 41.6 %all-to-all-start = ((bf16[2,16,32,512]{3,1,0,2:T(8,128)(2,1)}), bf16[2,16,32,512]{3,1,0,2:T(8,128)(2,1)S(1)}, u32[]{:S(2)}, u32[]{:S(2)}) async-start(bf16[2,16,32,512]{3,1,0,2:T(8,128)(2,1)} %bitcast.71), calls=%async_computation | async-start | bytes 2097152 | tf_op jit(solution)/shard_map/all_to_all | solution.py:40
  47.6 176.6 %all-gather.15.cloned.1.call-start = ((), (), s32[]{:S(2)}) async-start(), calls=%async_computation.5 | async-start | bytes 2162688 | tf_op jit(solution)/shard_map/all_gather | solution.py:57
  82.7 51.0 %copy-start.11 = (bf16[512,512]{1,0:T(8,128)(2,1)}, bf16[512,512]{1,0:T(8,128)(2,1)S(1)}, u32[]{:S(2)}) copy-start(bf16[512,512]{1,0:T(8,128)(2,1)S(1)} %get-tuple-element.16) | copy-start | bytes 1572868
  82.7 55.0 %copy-start.5 = (bf16[512,512]{1,0:T(8,128)(2,1)}, bf16[512,512]{1,0:T(8,128)(2,1)S(1)}, u32[]{:S(2)}) copy-start(bf16[512,512]{1,0:T(8,128)(2,1)S(1)} %get-tuple-element.11) | copy-start | bytes 1572868
  82.7 55.0 %copy-start.8 = (bf16[512,512]{1,0:T(8,128)(2,1)}, bf16[512,512]{1,0:T(8,128)(2,1)S(1)}, u32[]{:S(2)}) copy-start(bf16[512,512]{1,0:T(8,128)(2,1)S(1)} %get-tuple-element.17) | copy-start | bytes 1572868
  133.7 4.0 %copy-start.19 = (bf16[2,512,1024]{2,1,0:T(8,128)(2,1)S(1)}, bf16[2,512,1024]{2,1,0:T(8,128)(2,1)}, u32[]{:S(2)}) copy-start(bf16[2,512,1024]{2,1,0:T(8,128)(2,1)} %all-gather.7.cloned.1.call-done) | copy-start | bytes 6291460
  137.8 1.6 copy-start.17
  179.0 4.2 %copy-start.6 = (bf16[512,512]{1,0:T(8,128)(2,1)S(1)}, bf16[512,512]{1,0:T(8,128)(2,1)}, u32[]{:S(2)}) copy-start(bf16[512,512]{1,0:T(8,128)(2,1)} %copy-done.5) | copy-start | bytes 1572868
  179.0 4.2 %copy-start.9 = (bf16[512,512]{1,0:T(8,128)(2,1)S(1)}, bf16[512,512]{1,0:T(8,128)(2,1)}, u32[]{:S(2)}) copy-start(bf16[512,512]{1,0:T(8,128)(2,1)} %copy-done.8) | copy-start | bytes 1572868
  179.0 4.2 %copy-start.21 = (bf16[2,512,1024]{2,1,0:T(8,128)(2,1)S(1)}, bf16[2,512,1024]{2,1,0:T(8,128)(2,1)}, u32[]{:S(2)}) copy-start(bf16[2,512,1024]{2,1,0:T(8,128)(2,1)} %all-gather.13.cloned.1.call-done) | copy-start | bytes 6291460
  224.2 3.3 %copy-start.7 = (bf16[512,512]{1,0:T(8,128)(2,1)S(1)}, bf16[512,512]{1,0:T(8,128)(2,1)}, u32[]{:S(2)}) copy-start(bf16[512,512]{1,0:T(8,128)(2,1)} %copy-done.5) | copy-start | bytes 1572868
  224.2 3.3 %copy-start.10 = (bf16[512,512]{1,0:T(8,128)(2,1)S(1)}, bf16[512,512]{1,0:T(8,128)(2,1)}, u32[]{:S(2)}) copy-start(bf16[512,512]{1,0:T(8,128)(2,1)} %copy-done.8) | copy-start | bytes 1572868
  224.2 3.3 %copy-start.23 = (bf16[2,512,1024]{2,1,0:T(8,128)(2,1)S(1)}, bf16[2,512,1024]{2,1,0:T(8,128)(2,1)}, u32[]{:S(2)}) copy-start(bf16[2,512,1024]{2,1,0:T(8,128)(2,1)} %all-gather.15.cloned.1.call-done) | copy-start | bytes 6291460
  227.5 2.3 copy-start.3
  227.5 2.3 copy-start.18
  229.8 1.6 copy-start.22
  231.4 1.3 copy-start.4
  238.8 2.4 copy-start.20
  243.4 1.3 copy-start
  243.4 1.5 copy-start.1
  243.4 1.9 copy-start.2
Sparse Core Ops, SparseCore 0:
  10.2 26.4 all-gather.8
  39.7 48.6 all-gather.10
  90.8 42.9 all-gather.6
  136.0 42.9 all-gather.12
  181.2 42.9 all-gather.14
where the time goes:
time: 272 us
  waiting for transfers between devices  150 us (55%)
  matrix products  38.2 us (14%)
  blocking collectives  29 us (11%)
  other arithmetic  25.1 us (9%)
  between operations  16.5 us (6%)
  starting transfers between devices  8.64 us (3%)
  local copies, waits for them, and re-layouts  4.61 us (2%)
    all_gather x4, waiting for transfers between devices, on_device(): lax.all_gather(piece, 'col', axis=1, tiled=True).reshape(2 * pairs, step)  123 us
    dot_general x16, matrix products, contract(): lax.dot_general(left_side, right_side, (((0,), (0,)), ((), ())), preferre...  38.2 us
    all_gather x1, blocking collectives, on_device(): lax.all_gather(bands, 'col', axis=1, tiled=True).astype(jnp.int32)  29 us
    all_gather x1, waiting for transfers between devices, on_device(): spread = lax.all_gather(both, 'row', axis=2, tiled=True)  24.9 us
    another operation x2, other arithmetic, on_device(): chi_imag = jnp.stack([jnp.concatenate(p, axis=0) for p in imag_parts])  10.8 us
    another operation x2, other arithmetic, on_device(): chi_real = jnp.stack([jnp.concatenate(p, axis=0) for p in real_parts])  9.18 us
    all_to_all x1, starting transfers between devices, on_device(): lax.all_to_all(spread, 'col', split_axis=2, concat_axis=1, tiled=True)  8.44 us
  transfers between devices with their start and end apart: 6, of which 5 were waited for; matrix products, arithmetic and copies ran while one was open for 9% of the time, Pallas kernels for 0%

commit v1 on v0

--- a/solution.py
+++ b/solution.py
@@ -2,6 +2,14 @@
 import jax.numpy as jnp
 from jax import lax
 from jax.sharding import PartitionSpec as P
+
+
+def gather_from_all(array, axis, dim):
+    size = lax.axis_size(axis)
+    repeats = [size if d == dim else 1 for d in range(array.ndim)]
+    return lax.all_to_all(
+        jnp.tile(array, repeats), axis, split_axis=dim, concat_axis=dim, tiled=True
+    )
 
 
 def lookup(indices, table):
@@ -54,7 +62,7 @@
     imag_parts = [[] for _ in right_real]
     for chunk in range(CHUNKS):
         piece = both[:, :, chunk * step : (chunk + 1) * step]
-        left = lax.all_gather(piece, "col", axis=1, tiled=True).reshape(2 * pairs, step)
+        left = gather_from_all(piece, "col", 1).reshape(2 * pairs, step)
         for index in range(len(right_real)):
             real_parts[index].append(contract(left, right_real[index]).astype(jnp.bfloat16))
             imag_parts[index].append(contract(left, right_imag[index]).astype(jnp.bfloat16))

time: 272 us -> 272 us (level)
  waiting for transfers between devices: 150 us -> 113 us
  local copies, waits for them, and re-layouts: 4.61 us -> 29.5 us
  starting transfers between devices: 8.64 us -> 32.9 us
  matrix products: 38.2 us -> 28 us
    all_gather x4 -> x0, waiting for transfers between devices: 123 us -> none  [on_device(): lax.all_gather(piece, 'col', axis=1, tiled=True).reshape(2 * pairs, step)]
    all_to_all x0 -> x4, waiting for transfers between devices: none -> 84.9 us  [gather_from_all(): lax.all_to_all(jnp.tile(array, repeats), axis, split_axis=dim, concat_axi...]
    all_to_all x0 -> x4, starting transfers between devices: none -> 24.4 us  [gather_from_all(): lax.all_to_all(jnp.tile(array, repeats), axis, split_axis=dim, concat_axi...]
    another operation x0 -> x4, local copies, waits for them, and re-layouts: none -> 12.8 us  [gather_from_all(): jnp.tile(array, repeats)]
    all_to_all x0 -> x4, local copies, waits for them, and re-layouts: none -> 11.2 us  [gather_from_all(): lax.all_to_all(jnp.tile(array, repeats), axis, split_axis=dim, concat_axi...]
    dot_general x16, matrix products: 38.2 us -> 28 us  [contract(): lax.dot_general(left_side, right_side, (((0,), (0,)), ((), ())), preferre...]
    all_gather x1, waiting for transfers between devices: 24.9 us -> 27.7 us  [on_device(): spread = lax.all_gather(both, 'row', axis=2, tiled=True)]
  transfers between devices with their start and end apart: 6 -> 6, of which waited for: 5 -> 4; matrix products, arithmetic and copies ran while one was open for 9% -> 6% of each run, Pallas kernels for 0% -> 0%
where the time goes in v1:
time: 272 us; the launch traced here: 271 us
  waiting for transfers between devices  113 us (42%)
  starting transfers between devices  32.9 us (12%)
  local copies, waits for them, and re-layouts  29.5 us (11%)
  blocking collectives  28.7 us (11%)
  matrix products  28 us (10%)
  other arithmetic  22.7 us (8%)
  between operations  16.9 us (6%)
    all_to_all x4, waiting for transfers between devices, gather_from_all(): lax.all_to_all(jnp.tile(array, repeats), axis, split_axis=dim, concat_axi...  84.9 us
    all_gather x1, blocking collectives, on_device(): lax.all_gather(bands, 'col', axis=1, tiled=True).astype(jnp.int32)  28.7 us
    dot_general x16, matrix products, contract(): lax.dot_general(left_side, right_side, (((0,), (0,)), ((), ())), preferre...  28 us
    all_gather x1, waiting for transfers between devices, on_device(): spread = lax.all_gather(both, 'row', axis=2, tiled=True)  27.7 us
    all_to_all x4, starting transfers between devices, gather_from_all(): lax.all_to_all(jnp.tile(array, repeats), axis, split_axis=dim, concat_axi...  24.4 us
    another operation x4, local copies, waits for them, and re-layouts, gather_from_all(): jnp.tile(array, repeats)  12.8 us
    all_to_all x4, local copies, waits for them, and re-layouts, gather_from_all(): lax.all_to_all(jnp.tile(array, repeats), axis, split_axis=dim, concat_axi...  11.2 us
    another operation x2, other arithmetic, on_device(): chi_imag = jnp.stack([jnp.concatenate(p, axis=0) for p in imag_parts])  10.8 us
  transfers between devices with their start and end apart: 6, of which 4 were waited for; matrix products, arithmetic and copies ran while one was open for 6% of the time, Pallas kernels for 0%

profile of v1, /device:TPU:1, one launch (start us, length us, event | category | flops | bytes accessed | tf_op | source)
XLA Modules:
  0.0 271.2 jit_solution(8661834514672592818)
XLA Ops:
  7.2 0.9 fusion.6
  8.1 0.1 copy.52
  8.1 3.2 %tile.42 = bf16[2,32,16,1024]{3,0,2,1:T(2,128)(2,1)} broadcast(bf16[2,16,1024]{2,0,1:T(2,128)(2,1)S(1)} %copy.52), dimensions={0,2,3} | broadcast | bytes 2162688 | tf_op jit(solution)/shard_map/tile | solution.py:11
  11.4 8.6 %all-to-all-start.4 = ((bf16[2,512,1024]{2,0,1:T(2,128)(2,1)}), bf16[2,512,1024]{2,0,1:T(2,128)(2,1)S(1)}, u32[]{:S(2)}, u32[]{:S(2)}) async-start(bf16[2,512,1024]{2,0,1:T(2,128)(2,1)} %bitcast.78), calls=%async_computation.4 | async-start | bytes 4194304 | tf_op jit(solution)/shard_map/all_to_all | solution.py:10
  20.0 0.1 copy.50
  20.0 28.2 %all-to-all-done.4 = bf16[2,512,1024]{2,0,1:T(2,128)(2,1)S(1)} async-done(((bf16[2,512,1024]{2,0,1:T(2,128)(2,1)}), bf16[2,512,1024]{2,0,1:T(2,128)(2,1)S(1)}, u32[]{:S(2)}, u32[]{:S(2)}) %all-to-all-start.4) | async-done | bytes 2097184 | tf_op jit(solution)/shard_map/all_to_all | solution.py:10
  48.2 3.2 %tile.40 = bf16[2,32,16,1024]{3,0,2,1:T(2,128)(2,1)} broadcast(bf16[2,16,1024]{2,0,1:T(2,128)(2,1)S(1)} %copy.50), dimensions={0,2,3} | broadcast | bytes 2162688 | tf_op jit(solution)/shard_map/tile | solution.py:11
  51.5 5.2 %all-to-all-start.3 = ((bf16[2,512,1024]{2,0,1:T(2,128)(2,1)}), bf16[2,512,1024]{2,0,1:T(2,128)(2,1)}, u32[]{:S(2)}, u32[]{:S(2)}) async-start(bf16[2,512,1024]{2,0,1:T(2,128)(2,1)} %bitcast.79), calls=%async_computation.3 | async-start | bytes 4194304 | tf_op jit(solution)/shard_map/all_to_all | solution.py:10
  56.7 0.1 copy.48
  56.8 28.4 %all-to-all-done.3 = bf16[2,512,1024]{2,0,1:T(2,128)(2,1)} async-done(((bf16[2,512,1024]{2,0,1:T(2,128)(2,1)}), bf16[2,512,1024]{2,0,1:T(2,128)(2,1)}, u32[]{:S(2)}, u32[]{:S(2)}) %all-to-all-start.3) | async-done | bytes 2097184 | tf_op jit(solution)/shard_map/all_to_all | solution.py:10
  85.1 3.2 %tile.18 = bf16[2,32,16,1024]{3,0,2,1:T(2,128)(2,1)} broadcast(bf16[2,16,1024]{2,0,1:T(2,128)(2,1)S(1)} %copy.48), dimensions={0,2,3} | broadcast | bytes 2162688 | tf_op jit(solution)/shard_map/tile | solution.py:11
  88.3 5.2 %all-to-all-start.2 = ((bf16[2,512,1024]{2,0,1:T(2,128)(2,1)}), bf16[2,512,1024]{2,0,1:T(2,128)(2,1)}, u32[]{:S(2)}, u32[]{:S(2)}) async-start(bf16[2,512,1024]{2,0,1:T(2,128)(2,1)} %bitcast.77), calls=%async_computation.2 | async-start | bytes 4194304 | tf_op jit(solution)/shard_map/all_to_all | solution.py:10
  93.6 0.1 copy.42
  93.6 28.4 %all-to-all-done.2 = bf16[2,512,1024]{2,0,1:T(2,128)(2,1)} async-done(((bf16[2,512,1024]{2,0,1:T(2,128)(2,1)}), bf16[2,512,1024]{2,0,1:T(2,128)(2,1)}, u32[]{:S(2)}, u32[]{:S(2)}) %all-to-all-start.2) | async-done | bytes 2097184 | tf_op jit(solution)/shard_map/all_to_all | solution.py:10
  122.0 3.2 %tile.16 = bf16[2,32,16,1024]{3,0,2,1:T(2,128)(2,1)} broadcast(bf16[2,16,1024]{2,0,1:T(2,128)(2,1)S(1)} %copy.42), dimensions={0,2,3} | broadcast | bytes 2162688 | tf_op jit(solution)/shard_map/tile | solution.py:11
  125.2 5.4 %all-to-all-start = ((bf16[2,512,1024]{2,0,1:T(2,128)(2,1)}), bf16[2,512,1024]{2,0,1:T(2,128)(2,1)}, u32[]{:S(2)}, u32[]{:S(2)}) async-start(bf16[2,512,1024]{2,0,1:T(2,128)(2,1)} %bitcast.76), calls=%async_computation | async-start | bytes 4194304 | tf_op jit(solution)/shard_map/all_to_all | solution.py:10
  130.6 0.0 all-gather.3.cloned.1.call-start
  130.6 0.0 copy-done.4
  130.6 0.7 pad_maximum_fusion.6
  131.4 0.0 all-gather.3.cloned.1.call-update
  131.4 27.7 %all-gather.3.cloned.1.call-done = bf16[2,16,16384]{2,1,0:T(8,128)(2,1)} async-done(((bf16[2,16,4096]{2,1,0:T(8,128)(2,1)}), bf16[2,16,16384]{2,1,0:T(8,128)(2,1)}) %all-gather.3.cloned.1.call-update) | async-done | bytes 1048592 | tf_op jit(solution)/shard_map/all_gather | solution.py:46
  159.1 2.4 copy.57
  161.5 0.0 all-to-all-done
  161.5 8.4 %all-to-all-start.1 = ((bf16[2,16,32,512]{3,1,0,2:T(8,128)(2,1)}), bf16[2,16,32,512]{3,1,0,2:T(8,128)(2,1)S(1)}, u32[]{:S(2)}, u32[]{:S(2)}) async-start(bf16[2,16,32,512]{3,1,0,2:T(8,128)(2,1)} %bitcast.80), calls=%async_computation.1 | async-start | bytes 2097152 | tf_op jit(solution)/shard_map/all_to_all | solution.py:48
  169.9 0.6 fusion.17
  173.1 28.7 %all-gather = f32[32,16,2]{1,2,0:T(2,128)S(1)} all-gather(f32[1,16,2]{1,2,0:T(2,128)S(1)} %fusion.10), channel_id=1, replica_groups=mesh['row'=4,'col'=32] {'col'}, dimensions={0}, use_global_device_ids=true | all-gather | bytes 4224 | tf_op jit(solution)/shard_map/all_gather | solution.py:44
  201.9 0.1 copy.44
  202.0 0.1 copy.45
  202.1 0.1 reshape.73
  202.2 0.1 select_reduce_fusion.1
  202.3 0.1 select_reduce_fusion
  202.4 1.9 copy.53
  204.3 3.5 %copy.51 = bf16[2,512,1024]{2,1,0:T(8,128)(2,1)} copy(bf16[2,512,1024]{2,0,1:T(2,128)(2,1)} %all-to-all-done.3) | data formatting | bytes 4194304 | tf_op jit(solution)/shard_map/all_to_all | solution.py:10
  207.8 3.6 %copy.49 = bf16[2,512,1024]{2,1,0:T(8,128)(2,1)} copy(bf16[2,512,1024]{2,0,1:T(2,128)(2,1)} %all-to-all-done.2) | data formatting | bytes 4194304 | tf_op jit(solution)/shard_map/all_to_all | solution.py:10
  211.4 2.2 copy.43
  213.6 0.0 all-to-all-done.1
  213.6 0.3 convert_bitcast_fusion
  213.9 0.2 fusion.15
  214.1 0.0 copy-start.1
  214.1 0.4 fusion.5
  214.6 1.1 copy-done.1
  215.7 1.3 convolution_convert_fusion
  217.0 0.3 copy-done.2
  217.3 2.3 convolution_convert_fusion.1
  219.6 2.3 convolution_convert_fusion.4
  221.8 2.4 convolution_convert_fusion.5
  224.2 1.3 convolution_convert_fusion.8
  225.5 1.3 convolution_convert_fusion.9
  226.8 1.3 convolution_convert_fusion.12
  228.1 0.0 copy-start
  228.1 1.3 convolution_convert_fusion.13
  229.4 0.3 copy-done
  229.7 2.6 convolution_convert_fusion.2
  232.2 2.3 convolution_convert_fusion.6
  234.5 1.3 convolution_convert_fusion.10
  235.8 1.3 convolution_convert_fusion.14
  237.1 2.3 convolution_convert_fusion.3
  239.4 1.3 convolution_convert_fusion.11
  240.7 2.3 convolution_convert_fusion.7
  243.0 1.3 convolution_convert_fusion.15
  244.3 2.9 %maximum_bitcast_fusion = (bf16[1,4096,512]{2,1,0:T(8,128)(2,1)S(1)}, bf16[1,4096,512]{2,1,0:T(8,128)(2,1)}) fusion(bf16[1024,512]{1,0:T(8,128)(2,1)S(1)} %convolution_convert_fusion.12, bf16[1024,512]{1,0:T(8,128)(2,1)S(1)} %convolution_convert_fusion.13, bf16[1024,512]{1,0:T(8,128)(2,1)S(1)} %convolution_convert_fusion.14, ...), kind=kLoop, calls=%fused_computation.2 | loop fusion | flops 33554432 | bytes 16777216 | tf_op jit(solution)/shard_map/stack | solution.py:69
  247.2 6.4 %pad_maximum_fusion = bf16[2,4096,512]{2,1,0:T(8,128)(2,1)} fusion(bf16[1,4096,512]{2,1,0:T(8,128)(2,1)} %get-tuple-element.27, bf16[1,4096,512]{2,1,0:T(8,128)(2,1)S(1)} %get-tuple-element.26), kind=kLoop, calls=%fused_computation | loop fusion | flops 4194304 | bytes 16777216 | tf_op jit(solution)/shard_map/stack | solution.py:69
  253.6 4.5 %maximum_bitcast_fusion.2 = (bf16[1,4096,512]{2,1,0:T(8,128)(2,1)S(1)}, bf16[1,4096,512]{2,1,0:T(8,128)(2,1)}) fusion(bf16[1024,512]{1,0:T(8,128)(2,1)} %convolution_convert_fusion.4, bf16[1024,512]{1,0:T(8,128)(2,1)} %convolution_convert_fusion.5, bf16[1024,512]{1,0:T(8,128)(2,1)} %convolution_convert_fusion.6, ...), kind=kLoop, calls=%fused_computation.4 | loop fusion | flops 33554432 | bytes 16777216 | tf_op jit(solution)/shard_map/stack | solution.py:70
  258.0 6.3 %pad_maximum_fusion.1 = bf16[2,4096,512]{2,1,0:T(8,128)(2,1)} fusion(bf16[1,4096,512]{2,1,0:T(8,128)(2,1)} %get-tuple-element.29, bf16[1,4096,512]{2,1,0:T(8,128)(2,1)S(1)} %get-tuple-element.28), kind=kLoop, calls=%fused_computation.1 | loop fusion | flops 4194304 | bytes 16777216 | tf_op jit(solution)/shard_map/stack | solution.py:70
  (20 shorter events, 0.1 us)
Async XLA Ops:
  11.4 36.9 %all-to-all-start.4 = ((bf16[2,512,1024]{2,0,1:T(2,128)(2,1)}), bf16[2,512,1024]{2,0,1:T(2,128)(2,1)S(1)}, u32[]{:S(2)}, u32[]{:S(2)}) async-start(bf16[2,512,1024]{2,0,1:T(2,128)(2,1)} %bitcast.78), calls=%async_computation.4 | async-start | bytes 4194304 | tf_op jit(solution)/shard_map/all_to_all | solution.py:10
  51.5 33.7 %all-to-all-start.3 = ((bf16[2,512,1024]{2,0,1:T(2,128)(2,1)}), bf16[2,512,1024]{2,0,1:T(2,128)(2,1)}, u32[]{:S(2)}, u32[]{:S(2)}) async-start(bf16[2,512,1024]{2,0,1:T(2,128)(2,1)} %bitcast.79), calls=%async_computation.3 | async-start | bytes 4194304 | tf_op jit(solution)/shard_map/all_to_all | solution.py:10
  88.3 33.7 %all-to-all-start.2 = ((bf16[2,512,1024]{2,0,1:T(2,128)(2,1)}), bf16[2,512,1024]{2,0,1:T(2,128)(2,1)}, u32[]{:S(2)}, u32[]{:S(2)}) async-start(bf16[2,512,1024]{2,0,1:T(2,128)(2,1)} %bitcast.77), calls=%async_computation.2 | async-start | bytes 4194304 | tf_op jit(solution)/shard_map/all_to_all | solution.py:10
  125.2 5.4 %copy-start.4 = (bf16[16,4096]{1,0:T(8,128)(2,1)S(1)}, bf16[16,4096]{1,0:T(8,128)(2,1)}, u32[]{:S(2)}) copy-start(bf16[16,4096]{1,0:T(8,128)(2,1)} %param.7) | copy-start | bytes 393220
  125.2 5.4 %copy-start.5 = (bf16[16,4096]{1,0:T(8,128)(2,1)S(1)}, bf16[16,4096]{1,0:T(8,128)(2,1)}, u32[]{:S(2)}) copy-start(bf16[16,4096]{1,0:T(8,128)(2,1)} %param.8) | copy-start | bytes 393220
  125.2 36.3 %all-to-all-start = ((bf16[2,512,1024]{2,0,1:T(2,128)(2,1)}), bf16[2,512,1024]{2,0,1:T(2,128)(2,1)}, u32[]{:S(2)}, u32[]{:S(2)}) async-start(bf16[2,512,1024]{2,0,1:T(2,128)(2,1)} %bitcast.76), calls=%async_computation | async-start | bytes 4194304 | tf_op jit(solution)/shard_map/all_to_all | solution.py:10
  130.6 28.5 %all-gather.3.cloned.1.call-start = ((), (), s32[]{:S(2)}) async-start(), calls=%async_computation.5 | async-start | bytes 1310720 | tf_op jit(solution)/shard_map/all_gather | solution.py:46
  159.1 10.9 %copy-start.6 = (f32[2]{0:T(128)S(1)}, f32[2]{0:T(128)}, u32[]{:S(2)}) copy-start(f32[2]{0:T(128)} %param.13) | copy-start | bytes 28
  159.1 14.0 %copy-start.9 = (s32[16]{0:T(128)S(1)}, s32[16]{0:T(128)}, u32[]{:S(2)}) copy-start(s32[16]{0:T(128)} %param.10) | copy-start | bytes 196
  159.1 14.1 %copy-start.10 = (s32[16]{0:T(128)S(1)}, s32[16]{0:T(128)}, u32[]{:S(2)}) copy-start(s32[16]{0:T(128)} %param.9) | copy-start | bytes 196
  159.1 43.1 %copy-start.7 = (f32[16]{0:T(128)S(1)}, f32[16]{0:T(128)}, u32[]{:S(2)}) copy-start(f32[16]{0:T(128)} %param.11) | copy-start | bytes 196
  159.1 43.2 %copy-start.8 = (f32[32]{0:T(128)S(1)}, f32[32]{0:T(128)}, u32[]{:S(2)}) copy-start(f32[32]{0:T(128)} %param.12) | copy-start | bytes 388
  161.5 52.1 %all-to-all-start.1 = ((bf16[2,16,32,512]{3,1,0,2:T(8,128)(2,1)}), bf16[2,16,32,512]{3,1,0,2:T(8,128)(2,1)S(1)}, u32[]{:S(2)}, u32[]{:S(2)}) async-start(bf16[2,16,32,512]{3,1,0,2:T(8,128)(2,1)} %bitcast.80), calls=%async_computation.1 | async-start | bytes 2097152 | tf_op jit(solution)/shard_map/all_to_all | solution.py:48
  214.1 1.6 copy-start.1
  215.7 1.6 copy-start.2
  228.1 1.6 copy-start
  247.2 6.4 %copy-start.3 = (bf16[1024,512]{1,0:T(8,128)(2,1)S(1)}, bf16[1024,512]{1,0:T(8,128)(2,1)}, u32[]{:S(2)}) copy-start(bf16[1024,512]{1,0:T(8,128)(2,1)} %convolution_convert_fusion.1) | copy-start | bytes 3145732
Sparse Core Ops, SparseCore 0:
  133.6 25.3 all-gather.2
